TPU v7x, 32 devices: a whole 2x2x4 slice. The times are simulated.
32 devices in a mesh: parts: 2 (over y), filt: 4 (over z), space: 4 (over x, core).
Axes of the slice: x: 2, y: 2, z: 4, core: 2. Of those that a mesh axis runs over, the one named last changes fastest.
Arguments:
- volume: bfloat16 [512, 16, 8, 128], P('filt', ('parts', 'space')), parts along dimension 1, may hold values from -6 to 6
- weight: bfloat16 [512, 27, 512], P('filt'), may hold values from -0.0546875 to 0.0546875
- bias: float32 [512], P('filt'), may hold values from -3 to 3
- upstream: bfloat16 [512, 16, 8, 128], P('filt', ('parts', 'space')), parts along dimension 1, may hold values from -0.0625 to 0.0625
Outputs:
- features: bfloat16 [512, 16, 8, 128], P('filt', ('parts', 'space')), parts along dimension 1
- weight_grad: float32 [1024, 27, 512], P(('parts', 'filt')), parts along dimension 0
There are 2 independent parts, one for each index of `parts`. A program takes and returns all parts, laid end to end along the dimension named above; an argument that names none is the same for every part. Nothing has to cross between parts.
All inputs are finite; a program needn't handle non-finite values.
Results may differ from a plain program's by a relative error of at most 0.001.
Values may be sent and summed in bfloat16 or wider, within the bound.
No kernel may reach another device: no remote copies, remote signals or barrier semaphores. Data moves between devices by JAX's collectives and lax.ppermute only.
A program may use at most 128 MiB of HBM per device.

v0:
```python
import jax
import jax.numpy as jnp
from jax import lax
from jax.sharding import PartitionSpec as P


def padded(block, sides, width):
    for axis, dim in sides:
        count = lax.axis_size(axis)
        forward = [(i, i + 1) for i in range(count - 1)]
        backward = [(target, source) for source, target in forward]
        low = lax.ppermute(
            lax.slice_in_dim(block, block.shape[dim] - width, None, axis=dim), axis, forward
        )
        high = lax.ppermute(lax.slice_in_dim(block, 0, width, axis=dim), axis, backward)
        block = jnp.concatenate([low, block, high], axis=dim)
    return block


def convolve(slab, kernel):
    return lax.conv_general_dilated(
        slab[None],
        kernel,
        (1, 1, 1),
        [(0, 0), (1, 1), (1, 1)],
        dimension_numbers=("NCDHW", "OIDHW", "NCDHW"),
        preferred_element_type=jnp.float32,
    )[0]


def shifted_slopes(upstream):
    out_dev = upstream.shape[0]
    depth = upstream.shape[1]
    height = upstream.shape[2]
    length = upstream.shape[3]
    spread = jnp.pad(upstream, ((0, 0), (2, 2), (1, 1), (1, 1)))
    copies = []
    for tap in range(27):
        first = tap // 9
        second = tap // 3 % 3
        third = tap % 3
        copies.append(
            spread[
                :,
                2 - first : 4 - first + depth,
                2 - second : 2 - second + height,
                2 - third : 2 - third + length,
            ]
        )
    stacked = jnp.stack(copies, 1)
    return stacked.reshape(out_dev * 27, (depth + 2) * height * length)


def tap_grads(slab, slopes, out_dev):
    flat = slab.reshape(slab.shape[0], -1)
    product = lax.dot_general(
        slopes, flat, (((1,), (1,)), ((), ())), preferred_element_type=jnp.float32
    )
    return product.reshape(out_dev, 27, slab.shape[0])


def on_device(volume, weight, bias, upstream):
    out_dev = weight.shape[0]
    in_all = weight.shape[2]
    kernel = weight.reshape(out_dev, 3, 3, 3, in_all).transpose(0, 4, 1, 2, 3)
    slopes = shifted_slopes(upstream)
    whole = lax.all_gather(volume, "filt", axis=0, tiled=True)
    rimmed = padded(whole, (("space", 1),), 1)
    pre = convolve(rimmed, kernel)
    partial_grads = tap_grads(rimmed, slopes, out_dev)
    weight_grad = lax.psum(partial_grads, "space")
    pre = pre + bias[:, None, None, None]
    features = jnp.where(pre > 0, pre, 0.3 * pre).astype(jnp.bfloat16)
    return (features, weight_grad)


def solution(mesh):
    return jax.shard_map(
        on_device,
        mesh=mesh,
        in_specs=(
            P("filt", ("parts", "space"), None, None),
            P("filt", None, None),
            P("filt"),
            P("filt", ("parts", "space"), None, None),
        ),
        out_specs=(P("filt", ("parts", "space"), None, None), P(("parts", "filt"), None, None)),
        check_vma=False,
    )
```

profile of v0, /device:TPU:0, one launch (start us, length us, event | category | flops | bytes accessed | tf_op | source)
XLA Modules:
  0.0 254.6 jit_solution(8644923369791404062)
XLA Ops:
  7.2 2.1 copy.8
  20.5 1.4 fusion.35
  25.6 1.4 fusion.43
  34.4 24.5 %all-gather.2.cloned.1.call-done = bf16[512,2,8,128]{3,0,2,1:T(8,128)(2,1)} async-done(((bf16[128,2,8,128]{3,0,2,1:T(8,128)(2,1)}), bf16[512,2,8,128]{3,0,2,1:T(8,128)(2,1)}) %all-gather.2.cloned.1.call-update) | async-done | bytes 2097168 | tf_op jit(solution)/shard_map/all_gather | solution.py:67
  58.8 1.7 fusion.76
  60.5 1.8 collective-permute-start
  62.3 2.2 fusion.57
  64.5 2.3 fusion.59
  68.1 2.3 fusion.61
  70.4 2.2 fusion.63
  72.6 2.3 fusion.65
  75.0 2.4 fusion.67
  77.3 2.1 fusion.69
  79.5 2.3 fusion.71
  81.9 1.9 constant_dynamic-update-slice_fusion.1
  84.0 2.0 copy-done.2
  86.0 20.7 %fusion.10 = f32[128,27,512]{2,0,1:T(8,128)} fusion(bf16[128,27,4,8,128]{4,0,3,2,1:T(8,128)(2,1)} %fusion.71, bf16[512,4,8,128]{3,0,2,1:T(8,128)(2,1)S(1)} %constant_dynamic-update-slice_fusion), kind=kOutput, calls=%fused_computation.38 | convolution fusion | flops 14495514624 | bytes 39583744 | tf_op jit(solution)/shard_map/dot_general | solution.py:56
  106.7 8.0 %copy.18 = bf16[512,4,8,1,128]{0,2,4,1,3:T(8,128)(2,1)} copy(bf16[512,4,8,1,128]{4,0,2,1,3:T(8,128)(2,1)} %bitcast.144) | data formatting | bytes 8388608
  114.7 2.6 %pad.5.clone = bf16[512,4,8,1,136]{0,2,4,1,3:T(8,128)(2,1)S(1)} pad(bf16[512,4,8,1,128]{0,2,4,1,3:T(8,128)(2,1)} %copy.18, bf16[]{:T(256)} %constant.6.clone.1), padding=0_0x0_0x0_0x0_0x1_7 | pad | bytes 8650754 | tf_op jit(solution)/shard_map/broadcast_in_dim | solution.py:22
  117.3 1.7 copy.11
  119.2 16.9 %fusion.14 = f32[2,8,8,17,128]{4,2,3,1,0:T(8,128)S(1)} fusion(bf16[128,3,3,3,512]{4,0,3,2,1:T(8,128)(2,1)S(1)} %bitcast.142, bf16[512,4,8,1,7,2]{0,4,5,2,1,3:T(8,128)(2,1)S(1)} %slice.120, bf16[512,4,8,1,8,17]{0,4,5,2,1,3:T(8,128)(2,1)S(1)} %copy.11, pred[8,17]{0,1:T(8,128)(4,1)S(1)} %copy-done.4), kind=kOutput, calls=%fused_computation.40 | convolution fusion | flops 7074234368 | bytes 9568392 | tf_op jit(solution)/shard_map/conv_general_dilated | solution.py:21
  137.3 2.4 copy.14
  139.7 100.7 %all-reduce.3.cloned.1.call-done = f32[128,27,512]{2,0,1:T(8,128)} async-done(((f32[128,27,512]{2,0,1:T(8,128)}), f32[128,27,512]{2,0,1:T(8,128)}) %all-reduce.3.cloned.1.call-update) | async-done | bytes 7077904 | tf_op jit(solution)/shard_map/psum | solution.py:71
  240.4 7.3 %copy.48 = f32[128,27,512]{2,0,1:T(8,128)} copy(f32[128,27,512]{2,0,1:T(8,128)} %all-reduce.3.cloned.1.call-done) | data formatting | bytes 14155776
  (39 shorter events, 25.1 us)
Async XLA Ops:
  7.2 112.0 %copy-start = (bf16[128,27,512]{2,0,1:T(8,128)(2,1)S(1)}, bf16[128,27,512]{2,0,1:T(8,128)(2,1)}, u32[]{:S(2)}) copy-start(bf16[128,27,512]{2,0,1:T(8,128)(2,1)} %param.5) | copy-start | bytes 10616836
  7.2 51.7 %all-gather.2.cloned.1.call-start = ((), (), s32[]{:S(2)}) async-start(), calls=%async_computation | async-start | bytes 2621440 | tf_op jit(solution)/shard_map/all_gather | solution.py:67
  9.4 231.0 %all-reduce.3.cloned.1.call-start = ((), (), s32[]{:S(2)}) async-start(), calls=%async_computation.1 | async-start | bytes 14155776 | tf_op jit(solution)/shard_map/psum | solution.py:71
  10.6 22.5 %copy-start.1 = (bf16[128,2,8,128]{3,0,2,1:T(8,128)(2,1)}, bf16[128,2,8,128]{3,0,2,1:T(8,128)(2,1)S(1)}, u32[]{:S(2)}) copy-start(bf16[128,2,8,128]{3,0,2,1:T(8,128)(2,1)S(1)} %copy.13) | copy-start | bytes 1572868
  60.5 21.2 %collective-permute-start = (bf16[512,1,8,128]{3,0,2,1:T(8,128)(2,1)S(1)}, bf16[512,1,8,128]{3,0,2,1:T(8,128)(2,1)S(1)}, u32[]{:S(2)}, u32[]{:S(2)}) collective-permute-start(bf16[512,1,8,128]{3,0,2,1:T(8,128)(2,1)S(1)} %get-tuple-element.5), channel_id=1, source_target_pairs={{0,1},{1,2},{2,3},{4,5},{5,6},{6,7},{8,9},{9,10},{10,11},{12,13},{... | collective-permute-start | bytes 3145736 | tf_op jit(solution)/shard_map/ppermute | solution.py:12
  66.8 17.0 %collective-permute-start.1 = (bf16[512,1,8,128]{3,0,2,1:T(8,128)(2,1)S(1)}, bf16[512,1,8,128]{3,0,2,1:T(8,128)(2,1)S(1)}, u32[]{:S(2)}, u32[]{:S(2)}) collective-permute-start(bf16[512,1,8,128]{3,0,2,1:T(8,128)(2,1)S(1)} %get-tuple-element.4), channel_id=1, source_target_pairs={{1,0},{2,1},{3,2},{5,4},{6,5},{7,6},{9,8},{10,9},{11,10},{13,12},{... | collective-permute-start | bytes 3145736 | tf_op jit(solution)/shard_map/ppermute | solution.py:15
  83.9 2.0 copy-start.2
  106.6 12.6 %copy-start.4 = (pred[8,17]{0,1:T(8,128)(4,1)S(1)}, pred[8,17]{0,1:T(8,128)(4,1)}, u32[]{:S(2)}) copy-start(pred[8,17]{0,1:T(8,128)(4,1)} %constant.15) | copy-start | bytes 412
  119.2 17.1 %copy-start.3 = (f32[128]{0:T(128)S(1)}, f32[128]{0:T(128)}, u32[]{:S(2)}) copy-start(f32[128]{0:T(128)} %param.6) | copy-start | bytes 1540
Sparse Core Ops, SparseCore 0:
  10.2 48.6 all-gather.1
  106.8 133.5 all-reduce.2
where the time goes:
time: 255 us
  waiting for transfers between devices  125 us (49%)
  local copies, waits for them, and re-layouts  73.5 us (29%)
  matrix products  37.5 us (15%)
  between operations  14.2 us (6%)
  starting transfers between devices  3.13 us (1%)
    psum x1, waiting for transfers between devices, on_device(): weight_grad = lax.psum(partial_grads, 'space')  101 us
    unnamed x43, local copies, waits for them, and re-layouts  64.7 us
    all_gather x1, waiting for transfers between devices, on_device(): whole = lax.all_gather(volume, 'filt', axis=0, tiled=True)  24.5 us
    dot_general x1, matrix products, tap_grads(): lax.dot_general(slopes, flat, (((1,), (1,)), ((), ())), preferred_element...  20.7 us
    conv_general_dilated x1, matrix products, convolve(): lax.conv_general_dilated(slab[None], kernel, (1, 1, 1), [(0, 0), (1, 1),...  16.9 us
  transfers between devices with their start and end apart: 4, of which 2 were waited for; matrix products, arithmetic and copies ran while one was open for 31% of the time, Pallas kernels for 0%

commit v1 on v0

--- a/solution.py
+++ b/solution.py
@@ -68,7 +68,7 @@
     rimmed = padded(whole, (("space", 1),), 1)
     pre = convolve(rimmed, kernel)
     partial_grads = tap_grads(rimmed, slopes, out_dev)
-    weight_grad = lax.psum(partial_grads, "space")
+    weight_grad = jnp.sum(lax.all_gather(partial_grads, "space"), axis=0)
     pre = pre + bias[:, None, None, None]
     features = jnp.where(pre > 0, pre, 0.3 * pre).astype(jnp.bfloat16)
     return (features, weight_grad)

time: 255 us -> 303 us (1.19)
  waiting for transfers between devices: 125 us -> 164 us
  other arithmetic: 0.96 us -> 15.7 us
  local copies, waits for them, and re-layouts: 73.5 us -> 67 us
    all_gather x0 -> x1, waiting for transfers between devices: none -> 140 us  [on_device(): weight_grad = jnp.sum(lax.all_gather(partial_grads, 'space'), axis=0)]
    psum x1 -> x0, waiting for transfers between devices: 101 us -> none  [on_device(): weight_grad = lax.psum(partial_grads, 'space')]
    reduce_sum x0 -> x1, other arithmetic: none -> 14.8 us  [on_device(): weight_grad = jnp.sum(lax.all_gather(partial_grads, 'space'), axis=0)]
    unnamed x43 -> x42, local copies, waits for them, and re-layouts: 64.7 us -> 57.3 us
  transfers between devices with their start and end apart: 4 -> 4, of which waited for: 2 -> 2; matrix products, arithmetic and copies ran while one was open for 31% -> 26% of each run, Pallas kernels for 0% -> 0%
where the time goes in v1:
time: 303 us; the launch traced here: 302 us
  waiting for transfers between devices  164 us (54%)
  local copies, waits for them, and re-layouts  67 us (22%)
  matrix products  37.5 us (12%)
  other arithmetic  15.7 us (5%)
  between operations  14.2 us (5%)
  starting transfers between devices  3.13 us (1%)
    all_gather x1, waiting for transfers between devices, on_device(): weight_grad = jnp.sum(lax.all_gather(partial_grads, 'space'), axis=0)  140 us
    unnamed x42, local copies, waits for them, and re-layouts  57.3 us
    all_gather x1, waiting for transfers between devices, on_device(): whole = lax.all_gather(volume, 'filt', axis=0, tiled=True)  24.5 us
    dot_general x1, matrix products, tap_grads(): lax.dot_general(slopes, flat, (((1,), (1,)), ((), ())), preferred_element...  20.7 us
    conv_general_dilated x1, matrix products, convolve(): lax.conv_general_dilated(slab[None], kernel, (1, 1, 1), [(0, 0), (1, 1),...  16.9 us
    reduce_sum x1, other arithmetic, on_device(): weight_grad = jnp.sum(lax.all_gather(partial_grads, 'space'), axis=0)  14.8 us
  transfers between devices with their start and end apart: 4, of which 2 were waited for; matrix products, arithmetic and copies ran while one was open for 26% of the time, Pallas kernels for 0%

profile of v1, /device:TPU:0, one launch (start us, length us, event | category | flops | bytes accessed | tf_op | source)
XLA Modules:
  0.0 301.8 jit_solution(11401252176695299645)
XLA Ops:
  7.2 2.1 copy.8
  20.5 1.4 fusion.35
  25.6 1.4 fusion.43
  34.4 24.5 %all-gather.4.cloned.1.call-done = bf16[512,2,8,128]{3,0,2,1:T(8,128)(2,1)} async-done(((bf16[128,2,8,128]{3,0,2,1:T(8,128)(2,1)}), bf16[512,2,8,128]{3,0,2,1:T(8,128)(2,1)}) %all-gather.4.cloned.1.call-update) | async-done | bytes 2097168 | tf_op jit(solution)/shard_map/all_gather | solution.py:67
  58.8 1.7 fusion.76
  60.5 1.8 collective-permute-start
  62.3 2.2 fusion.57
  64.5 2.3 fusion.59
  68.1 2.3 fusion.61
  70.4 2.2 fusion.63
  72.6 2.3 fusion.65
  75.0 2.4 fusion.67
  77.3 2.1 fusion.69
  79.5 2.3 fusion.71
  81.9 1.9 constant_dynamic-update-slice_fusion.1
  84.0 2.0 copy-done.2
  86.0 20.7 %fusion.10 = f32[128,27,512]{2,0,1:T(8,128)} fusion(bf16[128,27,4,8,128]{4,0,3,2,1:T(8,128)(2,1)} %fusion.71, bf16[512,4,8,128]{3,0,2,1:T(8,128)(2,1)S(1)} %constant_dynamic-update-slice_fusion), kind=kOutput, calls=%fused_computation.38 | convolution fusion | flops 14495514624 | bytes 39583744 | tf_op jit(solution)/shard_map/dot_general | solution.py:56
  106.7 8.0 %copy.18 = bf16[512,4,8,1,128]{0,2,4,1,3:T(8,128)(2,1)} copy(bf16[512,4,8,1,128]{4,0,2,1,3:T(8,128)(2,1)} %bitcast.146) | data formatting | bytes 8388608
  114.6 3.6 %pad.5.clone = bf16[512,4,8,1,136]{0,2,4,1,3:T(8,128)(2,1)S(1)} pad(bf16[512,4,8,1,128]{0,2,4,1,3:T(8,128)(2,1)} %copy.18, bf16[]{:T(256)} %constant.2.clone.1), padding=0_0x0_0x0_0x0_0x1_7 | pad | bytes 8650754 | tf_op jit(solution)/shard_map/broadcast_in_dim | solution.py:22
  118.2 1.7 copy.11
  120.1 16.9 %fusion.14 = f32[2,8,8,17,128]{4,2,3,1,0:T(8,128)S(1)} fusion(bf16[128,3,3,3,512]{4,0,3,2,1:T(8,128)(2,1)S(1)} %bitcast.143, bf16[512,4,8,1,7,2]{0,4,5,2,1,3:T(8,128)(2,1)S(1)} %slice.120, bf16[512,4,8,1,8,17]{0,4,5,2,1,3:T(8,128)(2,1)S(1)} %copy.11, pred[8,17]{0,1:T(8,128)(4,1)S(1)} %copy-done.4), kind=kOutput, calls=%fused_computation.40 | convolution fusion | flops 7074234368 | bytes 9568392 | tf_op jit(solution)/shard_map/conv_general_dilated | solution.py:21
  138.2 2.4 copy.14
  140.6 139.7 %all-gather.6.cloned.1.call-done = f32[512,27,512]{2,0,1:T(8,128)} async-done(((f32[128,27,512]{2,0,1:T(8,128)}), f32[512,27,512]{2,0,1:T(8,128)}) %all-gather.6.cloned.1.call-update) | async-done | bytes 28311568 | tf_op jit(solution)/shard_map/all_gather | solution.py:71
  280.2 14.8 %reduce_sum.9 = f32[128,27,512]{2,0,1:T(8,128)} reduce(f32[4,128,27,512]{3,1,0,2:T(8,128)} %bitcast.144, f32[]{:T(128)} %constant.3.clone.1), dimensions={0}, to_apply=%region_0.1 | reduce | flops 5308416 | bytes 35389444 | tf_op jit(solution)/shard_map/reduce_sum | solution.py:71
  (39 shorter events, 25.1 us)
Async XLA Ops:
  7.2 112.9 %copy-start = (bf16[128,27,512]{2,0,1:T(8,128)(2,1)S(1)}, bf16[128,27,512]{2,0,1:T(8,128)(2,1)}, u32[]{:S(2)}) copy-start(bf16[128,27,512]{2,0,1:T(8,128)(2,1)} %param.5) | copy-start | bytes 10616836
  7.2 51.7 %all-gather.4.cloned.1.call-start = ((), (), s32[]{:S(2)}) async-start(), calls=%async_computation | async-start | bytes 2621440 | tf_op jit(solution)/shard_map/all_gather | solution.py:67
  9.4 270.9 %all-gather.6.cloned.1.call-start = ((), (), s32[]{:S(2)}) async-start(), calls=%async_computation.1 | async-start | bytes 35389440 | tf_op jit(solution)/shard_map/all_gather | solution.py:71
  10.6 22.5 %copy-start.1 = (bf16[128,2,8,128]{3,0,2,1:T(8,128)(2,1)}, bf16[128,2,8,128]{3,0,2,1:T(8,128)(2,1)S(1)}, u32[]{:S(2)}) copy-start(bf16[128,2,8,128]{3,0,2,1:T(8,128)(2,1)S(1)} %copy.13) | copy-start | bytes 1572868
  60.5 21.2 %collective-permute-start = (bf16[512,1,8,128]{3,0,2,1:T(8,128)(2,1)S(1)}, bf16[512,1,8,128]{3,0,2,1:T(8,128)(2,1)S(1)}, u32[]{:S(2)}, u32[]{:S(2)}) collective-permute-start(bf16[512,1,8,128]{3,0,2,1:T(8,128)(2,1)S(1)} %get-tuple-element.5), channel_id=1, source_target_pairs={{0,1},{1,2},{2,3},{4,5},{5,6},{6,7},{8,9},{9,10},{10,11},{12,13},{... | collective-permute-start | bytes 3145736 | tf_op jit(solution)/shard_map/ppermute | solution.py:12
  66.8 17.0 %collective-permute-start.1 = (bf16[512,1,8,128]{3,0,2,1:T(8,128)(2,1)S(1)}, bf16[512,1,8,128]{3,0,2,1:T(8,128)(2,1)S(1)}, u32[]{:S(2)}, u32[]{:S(2)}) collective-permute-start(bf16[512,1,8,128]{3,0,2,1:T(8,128)(2,1)S(1)} %get-tuple-element.4), channel_id=1, source_target_pairs={{1,0},{2,1},{3,2},{5,4},{6,5},{7,6},{9,8},{10,9},{11,10},{13,12},{... | collective-permute-start | bytes 3145736 | tf_op jit(solution)/shard_map/ppermute | solution.py:15
  83.9 2.0 copy-start.2
  106.6 13.4 %copy-start.4 = (pred[8,17]{0,1:T(8,128)(4,1)S(1)}, pred[8,17]{0,1:T(8,128)(4,1)}, u32[]{:S(2)}) copy-start(pred[8,17]{0,1:T(8,128)(4,1)} %constant.16) | copy-start | bytes 412
  120.1 17.1 %copy-start.3 = (f32[128]{0:T(128)S(1)}, f32[128]{0:T(128)}, u32[]{:S(2)}) copy-start(f32[128]{0:T(128)} %param.6) | copy-start | bytes 1540
Sparse Core Ops, SparseCore 0:
  10.2 48.6 all-gather.3
  106.8 173.4 all-gather.5
